TPU v7x, 32 devices: a whole 2x2x4 slice. The times are simulated.
32 devices in a mesh: dp: 8 (over z, core), tensor: 4 (over y, x).
Axes of the slice: x: 2, y: 2, z: 4, core: 2. Of those that a mesh axis runs over, the one named last changes fastest.
Arguments:
- t_index: int32 [8], P('dp'), may hold values from 0 to 999
- cond_slot: int32 [8], P('dp'), may hold values from 0 to 1
- positions: int32 [8, 3, 512], P('dp'), may hold values from 0 to 63, as said below
- latent: bfloat16 [8, 512, 5120], P('dp', 'tensor'), may hold values from -6 to 6
- teacher_query: bfloat16 [2, 8, 512, 4096], P(None, 'dp', None, 'tensor'), may hold values from -6 to 6
- teacher_key: bfloat16 [2, 8, 512, 4096], P(None, 'dp', None, 'tensor'), may hold values from -6 to 6
- teacher_value: bfloat16 [2, 8, 512, 4096], P(None, 'dp', None, 'tensor'), may hold values from -6 to 6
- student_query: bfloat16 [8, 512, 4096], P('dp', 'tensor'), may hold values from -6 to 6
- student_key: bfloat16 [8, 512, 4096], P('dp', 'tensor'), may hold values from -6 to 6
- student_value: bfloat16 [8, 512, 4096], P('dp', 'tensor'), may hold values from -6 to 6
- query_tangent: bfloat16 [8, 512, 4096], P('dp', 'tensor'), may hold values from -6 to 6
- key_tangent: bfloat16 [8, 512, 4096], P('dp', 'tensor'), may hold values from -6 to 6
- value_tangent: bfloat16 [8, 512, 4096], P('dp', 'tensor'), may hold values from -6 to 6
- teacher_out: bfloat16 [4096, 5120], P('tensor', 'dp'), may hold values from -0.375 to 0.375
- student_out: bfloat16 [4096, 5120], P('tensor', 'dp'), may hold values from -0.375 to 0.375
Outputs:
- target: bfloat16 [8, 512, 5120], P('dp', 'tensor')
- gradient: float32 [4096, 5120], P('tensor', 'dp')
Inputs may be any that keep to these rules, and one draw needn't show every extreme that they name: `positions`: within each clip, tokens 64 m and 64 m + 1 have equal coordinates on all three axes.
All inputs are finite; a program needn't handle non-finite values.
Results may differ from a plain program's by a relative error of at most 0.015.
Values may be sent and summed in bfloat16 or wider, within the bound.
No kernel may reach another device: no remote copies, remote signals or barrier semaphores. Data moves between devices by JAX's collectives and lax.ppermute only.
A program may use at most 192 MiB of HBM per device.

v0:
```python
import math
import jax
import jax.numpy as jnp
from jax import lax
from jax.sharding import PartitionSpec as P

HD = 128
STEPS = 1000
sigma_data = 0.5
guidance = 5.0


def rope_angles(coords):
    half_size = HD // 2
    sixth = HD // 6
    first_pairs = half_size - 2 * sixth
    pair_index = jnp.arange(half_size)
    axis_id = (pair_index >= first_pairs).astype(jnp.int32) + (
        pair_index >= first_pairs + sixth
    ).astype(jnp.int32)
    offset = jnp.where(axis_id == 0, 0, jnp.where(axis_id == 1, first_pairs, first_pairs + sixth))
    axis_width = jnp.where(axis_id == 0, 2 * first_pairs, 2 * sixth)
    exponent = 2.0 * (pair_index - offset).astype(jnp.float32) / axis_width.astype(jnp.float32)
    frequency = jnp.exp(-exponent * math.log(10000.0))
    angles = jnp.zeros((coords.shape[1], half_size), jnp.float32)
    for which_axis in range(3):
        chosen = jnp.where(axis_id == which_axis, frequency, 0.0)
        angles = angles + coords[which_axis].astype(jnp.float32)[:, None] * chosen[None, :]
    return angles


def rotate_heads(source, angles):
    half_size = source.shape[-1] // 2
    cos_angle = jnp.cos(angles)[:, None, :]
    sin_angle = jnp.sin(angles)[:, None, :]
    front_half = source[..., :half_size]
    back_half = source[..., half_size:]
    return jnp.concatenate(
        [
            front_half * cos_angle - back_half * sin_angle,
            back_half * cos_angle + front_half * sin_angle,
        ],
        axis=-1,
    )


def split_heads(source):
    return source.reshape(source.shape[0], -1, HD)


def rotated(source, angles):
    row_count = source.shape[0]
    return (
        rotate_heads(split_heads(source).astype(jnp.float32), angles)
        .astype(jnp.bfloat16)
        .reshape(row_count, -1)
    )


def softmax_rows(scores):
    row_peak = jnp.max(scores, axis=-1, keepdims=True)
    exponent = jnp.exp(scores - row_peak)
    return exponent / jnp.sum(exponent, axis=-1, keepdims=True)


def attend_plain(queries, key_rows, value_rows):
    scores = jnp.einsum(
        "qhd,khd->hqk", queries, key_rows, preferred_element_type=jnp.float32
    ) * HD ** (-0.5)
    rounded = softmax_rows(scores).astype(jnp.bfloat16)
    return jnp.einsum("hqk,khd->qhd", rounded, value_rows, preferred_element_type=jnp.float32)


def attend_tangent(queries, key_rows, value_rows, query_dir, key_dir, value_dir):
    score_scale = HD ** (-0.5)
    scores = (
        jnp.einsum("qhd,khd->hqk", queries, key_rows, preferred_element_type=jnp.float32)
        * score_scale
    )
    weights = softmax_rows(scores)
    rounded = weights.astype(jnp.bfloat16)
    primal = jnp.einsum("hqk,khd->qhd", rounded, value_rows, preferred_element_type=jnp.float32)
    score_dir = (
        jnp.einsum("qhd,khd->hqk", query_dir, key_rows, preferred_element_type=jnp.float32)
        + jnp.einsum("qhd,khd->hqk", queries, key_dir, preferred_element_type=jnp.float32)
    ) * score_scale
    weight_dir = weights * (score_dir - jnp.sum(weights * score_dir, axis=-1, keepdims=True))
    rounded_dir = weight_dir.astype(jnp.bfloat16)
    tangent = jnp.einsum(
        "hqk,khd->qhd", rounded_dir, value_rows, preferred_element_type=jnp.float32
    ) + jnp.einsum("hqk,khd->qhd", rounded, value_dir, preferred_element_type=jnp.float32)
    return (primal, tangent)


def local(
    t_index,
    cond_slot,
    positions,
    latent,
    teacher_query,
    teacher_key,
    teacher_value,
    student_query,
    student_key,
    student_value,
    query_tangent,
    key_tangent,
    value_tangent,
    teacher_out,
    student_out,
):
    groups = lax.axis_size("tensor")
    seq_local = latent.shape[1]
    seq_whole = seq_local * groups
    row_start = lax.axis_index("tensor") * seq_local
    time_value = 0.2 + 1.2 * (t_index[0].astype(jnp.float32) + 0.5) / STEPS
    cos_time = jnp.cos(time_value)
    sin_time = jnp.sin(time_value)
    angles_whole = rope_angles(positions[0])
    angles_local = lax.dynamic_slice_in_dim(angles_whole, row_start, seq_local, 0)
    outgoing = (
        rotated(student_query[0], angles_local),
        rotated(student_key[0], angles_local),
        student_value[0],
        rotated(query_tangent[0], angles_local),
        rotated(key_tangent[0], angles_local),
        value_tangent[0],
    )
    arrived = (
        lax.all_to_all(outgoing[0], "tensor", split_axis=1, concat_axis=0, tiled=True),
        lax.all_to_all(outgoing[1], "tensor", split_axis=1, concat_axis=0, tiled=True),
        lax.all_to_all(outgoing[2], "tensor", split_axis=1, concat_axis=0, tiled=True),
        lax.all_to_all(outgoing[3], "tensor", split_axis=1, concat_axis=0, tiled=True),
        lax.all_to_all(outgoing[4], "tensor", split_axis=1, concat_axis=0, tiled=True),
        lax.all_to_all(outgoing[5], "tensor", split_axis=1, concat_axis=0, tiled=True),
    )
    outputs = []
    for stream in range(2):
        outputs.append(
            attend_plain(
                split_heads(rotated(teacher_query[stream, 0], angles_whole)),
                split_heads(rotated(teacher_key[stream, 0], angles_whole)),
                split_heads(teacher_value[stream, 0]),
            )
        )
    cond_index = cond_slot[0]
    cond_out = jnp.where(cond_index == 0, outputs[0], outputs[1])
    uncond_out = jnp.where(cond_index == 0, outputs[1], outputs[0])
    teacher_term = (
        (cos_time * cos_time * sigma_data * (uncond_out + guidance * (cond_out - uncond_out)))
        .astype(jnp.bfloat16)
        .reshape(seq_whole, -1)
    )
    primal, tangent = attend_tangent(
        split_heads(arrived[0]),
        split_heads(arrived[1]),
        split_heads(arrived[2]),
        split_heads(arrived[3]),
        split_heads(arrived[4]),
        split_heads(arrived[5]),
    )
    student_term = (
        (-(cos_time * cos_time) * sigma_data * primal - cos_time * sin_time * sigma_data * tangent)
        .astype(jnp.bfloat16)
        .reshape(seq_whole, -1)
    )
    attended = primal.astype(jnp.bfloat16).reshape(seq_whole, -1)
    stacked = jnp.stack([student_out, teacher_out])
    pieces = lax.all_gather(stacked, "dp", axis=2, tiled=True)
    partial_value = jnp.dot(student_term, pieces[0], preferred_element_type=jnp.float32) + jnp.dot(
        teacher_term, pieces[1], preferred_element_type=jnp.float32
    )
    latent_weight = cos_time * sin_time
    clips = lax.axis_size("dp")
    copies = jnp.broadcast_to(attended[None], (clips,) + attended.shape)
    attended_all = lax.all_to_all(copies, "dp", split_axis=0, concat_axis=0, tiled=True)
    velocity = lax.psum_scatter(
        partial_value.astype(jnp.bfloat16), "tensor", scatter_dimension=0, tiled=True
    )
    velocity, attended_all = lax.optimization_barrier((velocity, attended_all))
    target = (velocity.astype(jnp.float32) - latent_weight * latent[0].astype(jnp.float32)).astype(
        jnp.bfloat16
    )
    width = target.shape[1] // clips
    columns = lax.all_to_all(
        target.reshape(seq_local, clips, width), "dp", split_axis=1, concat_axis=1, tiled=True
    )
    columns = lax.all_gather(columns, "tensor", axis=0, tiled=True)
    grad_scale = -2.0 / math.sqrt(clips * seq_whole)
    terms = jnp.einsum("csi,scd->cid", attended_all, columns, preferred_element_type=jnp.float32)
    gradient = jnp.sum((grad_scale * terms).astype(jnp.bfloat16).astype(jnp.float32), axis=0)
    return (target[None], gradient)


def solution(mesh):
    placed = (
        P("dp"),
        P("dp"),
        P("dp", None, None),
        P("dp", "tensor", None),
        P(None, "dp", None, "tensor"),
        P(None, "dp", None, "tensor"),
        P(None, "dp", None, "tensor"),
        P("dp", "tensor", None),
        P("dp", "tensor", None),
        P("dp", "tensor", None),
        P("dp", "tensor", None),
        P("dp", "tensor", None),
        P("dp", "tensor", None),
        P("tensor", "dp"),
        P("tensor", "dp"),
    )
    return jax.shard_map(
        local,
        mesh=mesh,
        in_specs=placed,
        out_specs=(P("dp", "tensor", None), P("tensor", "dp")),
        check_vma=False,
    )
```

profile of v0, /device:TPU:0, one launch (start us, length us, event | category | flops | bytes accessed | tf_op | source)
XLA Modules:
  0.0 523.6 jit_solution(12055977299198744937)
XLA Ops:
  7.2 3.6 pad_maximum_fusion
  19.1 6.6 %subtract_convert_fusion.5 = (bf16[128,32,64]{0,2,1:T(8,128)(2,1)}, bf16[128,32,64]{0,2,1:T(8,128)(2,1)}, bf16[128,32,64]{0,2,1:T(8,128)(2,1)}, bf16[128,32,64]{...) fusion(f32[128,32,128]{0,2,1:T(8,128)} %bitcast.104, ...), kind=kLoop, calls=%fused_computation.76 | loop fusion | flops 8388608 | bytes 12648448 | tf_op jit(solution)/shard_map/convert.16
  26.7 5.3 %all-to-all-start = ((bf16[128,4,1024]{0,2,1:T(8,128)(2,1)}), bf16[128,4,1024]{0,2,1:T(8,128)(2,1)}, u32[]{:S(2)}, u32[]{:S(2)}) async-start(bf16[128,4,1024]{0,2,1:T(8,128)(2,1)} %bitcast.5), calls=%async_computation | async-start | bytes 2097152 | tf_op jit(solution)/shard_map/all_to_all | solution.py:130
  49.1 3.2 copy.182
  52.3 3.2 copy.183
  77.9 4.2 all-to-all-start.1
  82.2 8.8 %subtract_convert_fusion = (bf16[512,8,64]{2,0,1:T(8,128)(2,1)S(1)}, bf16[512,8,64]{2,0,1:T(8,128)(2,1)}, bf16[512,8,64]{2,0,1:T(8,128)(2,1)}, bf16[512,8,64]{2,...) fusion(f32[512,8,64]{2,0,1:T(8,128)} %copy.189, ...), kind=kLoop, calls=%fused_computation.41 | loop fusion | flops 8388608 | bytes 12845056 | tf_op jit(solution)/shard_map/convert.8
  90.9 5.4 %all-to-all-done.1 = bf16[128,4,1024]{0,2,1:T(8,128)(2,1)} async-done(((bf16[128,4,1024]{0,2,1:T(8,128)(2,1)}), bf16[128,4,1024]{0,2,1:T(8,128)(2,1)}, u32[]{:S(2)}, u32[]{:S(2)}) %all-to-all-start.1) | async-done | bytes 1048608 | tf_op jit(solution)/shard_map/all_to_all | solution.py:131
  96.3 4.8 all-to-all-start.3
  101.1 7.0 %fusion.30 = f32[8,512,512]{1,2,0:T(8,128)} fusion(bf16[512,8,64]{2,0,1:T(8,128)(2,1)} %get-tuple-element.40, bf16[512,8,64]{2,0,1:T(8,128)(2,1)} %get-tuple-element.41, bf16[512,8,64]{2,0,1:T(8,128)(2,1)} %get-tuple-element.36, bf16[512,8,64]{2,0,1:T(8,128)(2,1)} %get-tuple-element.37), kind=kOutput, calls=%fused_computation.58 | convolution fusion | flops 541065216 | bytes 10485760 | tf_op jit(solution)/shard_map/qhd,khd->hqk/dot_general | solution.py:67
  110.6 8.0 %fusion.97 = f32[8,512]{1,0:T(8,128)S(1)} fusion(f32[8,512,512]{1,2,0:T(8,128)} %fusion.30), kind=kOutput, calls=%fused_computation.125 | output fusion | flops 8389119 | bytes 8404992 | tf_op jit(solution)/shard_map/sub | solution.py:62
  118.6 4.3 all-to-all-start.4
  125.5 3.3 copy-done.1
  131.1 5.0 all-to-all-done.4
  136.1 4.4 all-to-all-start.2
  146.1 10.2 %fusion.19 = f32[8,512,128]{1,2,0:T(8,128)} fusion(bf16[512,8,128]{0,2,1:T(8,128)(2,1)S(1)} %bitcast.125, f32[8,512]{1,0:T(8,128)S(1)} %fusion.97, f32[8,512,512]{1,2,0:T(8,128)} %fusion.30), kind=kOutput, calls=%fused_computation.30 | convolution fusion | flops 547361280 | bytes 11550720 | tf_op jit(solution)/shard_map/hqk,khd->qhd/dot_general | solution.py:71
  156.3 10.8 %fusion.25 = bf16[512,8,128]{0,2,1:T(8,128)(2,1)} fusion(f32[8,512,128]{1,2,0:T(8,128)} %fusion.19, f32[]{:T(128)} %bitcast.26, pred[]{:T(512)} %bitcast.27, bf16[512,8,128]{0,2,1:T(8,128)(2,1)S(1)} %bitcast.124, f32[8,512]{1,0:T(8,128)S(1)} %fusion.98, f32[8,512,512]{1,2,0:T(8,128)} %copy-done.1), kind=kOutput, calls=%fused_computation.39 | convolution fusion | flops 551031296 | bytes 12599301 | tf_op jit(solution)/shard_map/hqk,khd->qhd/dot_general | solution.py:71
  179.2 4.5 all-to-all-start.5
  190.3 5.0 fusion.99
  196.2 10.9 %fusion.100 = (bf16[8,512,128]{1,2,0:T(8,128)(2,1)}, f32[8,512,128]{1,2,0:T(8,128)}) fusion(bf16[512,8,128]{0,2,1:T(8,128)(2,1)} %reshape.307, f32[8,512]{1,0:T(8,128)S(1)} %get-tuple-element.56, f32[8,512,512]{1,2,0:T(8,128)} %copy-done), kind=kOutput, calls=%fused_computation.128 | convolution fusion | flops 547885568 | bytes 12599296 | tf_op jit(solution)/shard_map/hqk,khd->qhd/dot_general | solution.py:82
  207.1 4.5 fusion.45
  211.6 5.3 %broadcast_in_dim.28 = bf16[8,512,1024]{1,2,0:T(8,128)(2,1)} broadcast(bf16[512,1024]{0,1:T(8,128)(2,1)} %bitcast.122), dimensions={1,2} | broadcast | bytes 9437184 | tf_op jit(solution)/shard_map/broadcast_in_dim | solution.py:175
  216.9 5.1 all-to-all-start.6
  222.1 10.0 %multiply_reduce_fusion = (f32[8,512]{1,0:T(8,128)S(1)}, f32[8,512,512]{1,2,0:T(8,128)}) fusion(f32[8,512,512]{1,2,0:T(8,128)} %get-tuple-element.57, f32[8,512]{1,0:T(8,128)S(1)} %get-tuple-element.56, f32[8,512,512]{1,2,0:T(8,128)} %fusion.45, bf16[512,8,128]{2,1,0:T(8,128)(2,1)S(1)} %bitcast.123, bf16[512,8,128]{2,1,0:T(8,128)(2,1)S(1)} %bitcast.110), kind=kOutput, calls=%fused_computation.15 | convolution fusion | flops 547352576 | bytes 27295744 | tf_op jit(solution)/shard_map/qhd,khd->hqk/dot_general | solution.py:85
  234.6 10.2 %fusion.28 = f32[8,512,128]{1,2,0:T(8,128)} fusion(bf16[512,8,128]{0,2,1:T(8,128)(2,1)S(1)} %reshape.310, f32[8,512]{1,0:T(8,128)S(1)} %get-tuple-element.56, f32[8,512,512]{1,2,0:T(8,128)} %copy-done), kind=kOutput, calls=%fused_computation.51 | convolution fusion | flops 547361280 | bytes 11550720 | tf_op jit(solution)/shard_map/hqk,khd->qhd/dot_general | solution.py:91
  244.9 11.5 %subtract_convert_fusion.4 = bf16[8,512,128]{1,2,0:T(8,128)(2,1)S(1)} fusion(f32[8,512,128]{1,2,0:T(8,128)} %fusion.28, f32[8,512,128]{1,2,0:T(8,128)} %get-tuple-element.61, bf16[512,8,128]{0,2,1:T(8,128)(2,1)S(1)} %copy-done.16, f32[8,512,512]{1,2,0:T(8,128)} %get-tuple-element.59, f32[8,512]{1,0:T(8,128)S(1)} %get-tuple-element.58, f32[]{:T(128)S(6)} %mul.409, ...), kind=kOutput, calls=%fused_computation.48 | convolution fusion | flops 554177024 | bytes 23101448 | tf_op jit(solution)/shard_map/hqk,khd->qhd/dot_general | solution.py:89
  256.5 8.4 %fusion.3 = f32[512,5120]{1,0:T(8,128)S(1)} fusion(bf16[512,1024]{0,1:T(8,128)(2,1)S(1)} %bitcast.119, bf16[2,1024,5120]{2,1,0:T(8,128)(2,1)} %all-gather.3.cloned.1.call-done), kind=kOutput, calls=%fused_computation.6 | convolution fusion | flops 5368709120 | bytes 22020096 | tf_op jit(solution)/shard_map/dot_general | solution.py:170
  264.8 12.0 %add_convert_fusion = bf16[512,5120]{1,0:T(8,128)(2,1)} fusion(f32[512,5120]{1,0:T(8,128)S(1)} %fusion.3, bf16[512,1024]{0,1:T(8,128)(2,1)S(1)} %bitcast.126, bf16[2,1024,5120]{2,1,0:T(8,128)(2,1)} %all-gather.3.cloned.1.call-done), kind=kOutput, calls=%fused_computation.9 | convolution fusion | flops 5373952000 | bytes 27262976 | tf_op jit(solution)/shard_map/dot_general | solution.py:170
  277.2 128.8 %all-to-all-done.6 = bf16[8,512,1024]{1,2,0:T(8,128)(2,1)} async-done(((bf16[8,512,1024]{1,2,0:T(8,128)(2,1)}), bf16[8,512,1024]{1,2,0:T(8,128)(2,1)}, u32[]{:S(2)}, u32[]{:S(2)}) %all-to-all-start.6) | async-done | bytes 8388640 | tf_op jit(solution)/shard_map/all_to_all | solution.py:176
  407.8 35.4 %all_to_all.94 = bf16[128,8,640]{2,0,1:T(8,128)(2,1)} all-to-all(bf16[128,8,640]{2,0,1:T(8,128)(2,1)S(1)} %bitcast.108), channel_id=1, replica_groups=mesh['dp'=8,'tensor'=4] {'dp'}, dimensions={1} | all-to-all | bytes 2621440 | tf_op jit(solution)/shard_map/all_to_all | solution.py:185
  443.2 61.0 %all-gather.5.cloned.1.call-done = bf16[512,8,640]{2,0,1:T(8,128)(2,1)} async-done(((bf16[128,8,640]{2,0,1:T(8,128)(2,1)}), bf16[512,8,640]{2,0,1:T(8,128)(2,1)}) %all-gather.5.cloned.1.call-update) | async-done | bytes 5242896 | tf_op jit(solution)/shard_map/all_gather | solution.py:188
  504.2 12.3 %convert_reduce_fusion = f32[1024,640]{1,0:T(8,128)} fusion(bf16[8,512,1024]{1,2,0:T(8,128)(2,1)} %all-to-all-done.6, bf16[512,8,640]{2,0,1:T(8,128)(2,1)} %all-gather.5.cloned.1.call-done), kind=kOutput, calls=%fused_computation.3 | convolution fusion | flops 5389025280 | bytes 16252928 | tf_op jit(solution)/shard_map/csi,scd->cid/dot_general | solution.py:190
  (100 shorter events, 84.4 us)
Async XLA Ops:
  7.2 3.6 copy-start.11
  7.2 249.3 %all-gather.3.cloned.1.call-start = ((), (), s32[]{:S(2)}) async-start(), calls=%async_computation.9 | async-start | bytes 23592960 | tf_op jit(solution)/shard_map/all_gather | solution.py:169
  11.3 5.3 %copy-start.12 = (bf16[1,128,4096]{2,1,0:T(8,128)(2,1)S(1)}, bf16[1,128,4096]{2,1,0:T(8,128)(2,1)}, u32[]{:S(2)}) copy-start(bf16[1,128,4096]{2,1,0:T(8,128)(2,1)} %param.23) | copy-start | bytes 3145732
  11.4 7.0 %copy-start.17 = (s32[1,3,512]{2,0,1:T(1,128)S(1)}, s32[1,3,512]{2,0,1:T(1,128)}, u32[]{:S(2)}) copy-start(s32[1,3,512]{2,0,1:T(1,128)} %param.17) | copy-start | bytes 18436
  26.7 51.2 %all-to-all-start = ((bf16[128,4,1024]{0,2,1:T(8,128)(2,1)}), bf16[128,4,1024]{0,2,1:T(8,128)(2,1)}, u32[]{:S(2)}, u32[]{:S(2)}) async-start(bf16[128,4,1024]{0,2,1:T(8,128)(2,1)} %bitcast.5), calls=%async_computation | async-start | bytes 2097152 | tf_op jit(solution)/shard_map/all_to_all | solution.py:130
  68.1 8.7 %copy-start.7 = (bf16[128,32,64]{0,2,1:T(8,128)(2,1)S(1)}, bf16[128,32,64]{0,2,1:T(8,128)(2,1)}, u32[]{:S(2)}) copy-start(bf16[128,32,64]{0,2,1:T(8,128)(2,1)} %get-tuple-element.46) | copy-start | bytes 1572868
  68.1 8.7 %copy-start.8 = (bf16[128,32,64]{0,2,1:T(8,128)(2,1)S(1)}, bf16[128,32,64]{0,2,1:T(8,128)(2,1)}, u32[]{:S(2)}) copy-start(bf16[128,32,64]{0,2,1:T(8,128)(2,1)} %get-tuple-element.47) | copy-start | bytes 1572868
  77.9 18.4 %all-to-all-start.1 = ((bf16[128,4,1024]{0,2,1:T(8,128)(2,1)}), bf16[128,4,1024]{0,2,1:T(8,128)(2,1)}, u32[]{:S(2)}, u32[]{:S(2)}) async-start(bf16[128,4,1024]{0,2,1:T(8,128)(2,1)} %bitcast.8), calls=%async_computation.1 | async-start | bytes 2097152 | tf_op jit(solution)/shard_map/all_to_all | solution.py:131
  96.3 22.3 %all-to-all-start.3 = ((bf16[128,4,1024]{0,2,1:T(8,128)(2,1)}), bf16[128,4,1024]{0,2,1:T(8,128)(2,1)}, u32[]{:S(2)}, u32[]{:S(2)}) async-start(bf16[128,4,1024]{0,2,1:T(8,128)(2,1)} %bitcast.113), calls=%async_computation.3 | async-start | bytes 2097152 | tf_op jit(solution)/shard_map/all_to_all | solution.py:133
  101.1 7.1 %copy-start.13 = (bf16[1,128,4096]{2,1,0:T(8,128)(2,1)S(1)}, bf16[1,128,4096]{2,1,0:T(8,128)(2,1)}, u32[]{:S(2)}) copy-start(bf16[1,128,4096]{2,1,0:T(8,128)(2,1)} %param.24) | copy-start | bytes 3145732
  101.1 8.4 %copy-start.5 = (bf16[128,32,64]{0,2,1:T(8,128)(2,1)S(1)}, bf16[128,32,64]{0,2,1:T(8,128)(2,1)}, u32[]{:S(2)}) copy-start(bf16[128,32,64]{0,2,1:T(8,128)(2,1)} %get-tuple-element.14) | copy-start | bytes 1572868
  101.1 8.4 %copy-start.6 = (bf16[128,32,64]{0,2,1:T(8,128)(2,1)S(1)}, bf16[128,32,64]{0,2,1:T(8,128)(2,1)}, u32[]{:S(2)}) copy-start(bf16[128,32,64]{0,2,1:T(8,128)(2,1)} %get-tuple-element.15) | copy-start | bytes 1572868
  110.6 12.3 %copy-start.3 = (bf16[512,8,64]{2,0,1:T(8,128)(2,1)S(1)}, bf16[512,8,64]{2,0,1:T(8,128)(2,1)}, u32[]{:S(2)}) copy-start(bf16[512,8,64]{2,0,1:T(8,128)(2,1)} %get-tuple-element.7) | copy-start | bytes 1572868
  110.6 12.3 %copy-start.4 = (bf16[512,8,64]{2,0,1:T(8,128)(2,1)S(1)}, bf16[512,8,64]{2,0,1:T(8,128)(2,1)}, u32[]{:S(2)}) copy-start(bf16[512,8,64]{2,0,1:T(8,128)(2,1)} %get-tuple-element.38) | copy-start | bytes 1572868
  118.6 17.4 %all-to-all-start.4 = ((bf16[128,4,1024]{0,2,1:T(8,128)(2,1)}), bf16[128,4,1024]{0,2,1:T(8,128)(2,1)}, u32[]{:S(2)}, u32[]{:S(2)}) async-start(bf16[128,4,1024]{0,2,1:T(8,128)(2,1)} %bitcast.114), calls=%async_computation.4 | async-start | bytes 2097152 | tf_op jit(solution)/shard_map/all_to_all | solution.py:134
  125.5 3.3 copy-start.1
  131.1 11.9 %copy-start.14 = (bf16[1,128,4096]{2,1,0:T(8,128)(2,1)S(1)}, bf16[1,128,4096]{2,1,0:T(8,128)(2,1)}, u32[]{:S(2)}) copy-start(bf16[1,128,4096]{2,1,0:T(8,128)(2,1)} %param.27) | copy-start | bytes 3145732
  136.1 43.1 %all-to-all-start.2 = ((bf16[128,4,1024]{0,2,1:T(8,128)(2,1)}), bf16[128,4,1024]{0,2,1:T(8,128)(2,1)}, u32[]{:S(2)}, u32[]{:S(2)}) async-start(bf16[128,4,1024]{0,2,1:T(8,128)(2,1)} %bitcast.10), calls=%async_computation.2 | async-start | bytes 2097152 | tf_op jit(solution)/shard_map/all_to_all | solution.py:132
  179.2 32.4 %all-to-all-start.5 = ((bf16[128,4,1024]{0,2,1:T(8,128)(2,1)}), bf16[128,4,1024]{0,2,1:T(8,128)(2,1)}, u32[]{:S(2)}, u32[]{:S(2)}) async-start(bf16[128,4,1024]{0,2,1:T(8,128)(2,1)} %bitcast.112), calls=%async_computation.5 | async-start | bytes 2097152 | tf_op jit(solution)/shard_map/all_to_all | solution.py:135
  190.3 5.9 %copy-start = (f32[8,512,512]{1,2,0:T(8,128)}, f32[8,512,512]{1,2,0:T(8,128)S(1)}, u32[]{:S(2)}) copy-start(f32[8,512,512]{1,2,0:T(8,128)S(1)} %fusion.48) | copy-start | bytes 25165828
  216.9 5.2 copy-start.15
  216.9 189.0 %all-to-all-start.6 = ((bf16[8,512,1024]{1,2,0:T(8,128)(2,1)}), bf16[8,512,1024]{1,2,0:T(8,128)(2,1)}, u32[]{:S(2)}, u32[]{:S(2)}) async-start(bf16[8,512,1024]{1,2,0:T(8,128)(2,1)} %broadcast_in_dim.28), calls=%async_computation.7 | async-start | bytes 16777216 | tf_op jit(solution)/shard_map/all_to_all | solution.py:176
  222.1 183.9 %reduce-scatter.2.cloned.1.call-start = ((), (), s32[]{:S(2)}) async-start(), calls=%async_computation.10 | async-start | bytes 6553600 | tf_op jit(solution)/shard_map/reduce_scatter | solution.py:177
  234.6 10.3 %copy-start.16 = (bf16[512,8,128]{0,2,1:T(8,128)(2,1)S(1)}, bf16[512,8,128]{0,2,1:T(8,128)(2,1)}, u32[]{:S(2)}) copy-start(bf16[512,8,128]{0,2,1:T(8,128)(2,1)} %reshape.307) | copy-start | bytes 3145732
  244.9 11.6 %copy-start.9 = (bf16[512,8,128]{0,2,1:T(8,128)(2,1)S(1)}, bf16[512,8,128]{0,2,1:T(8,128)(2,1)}, u32[]{:S(2)}) copy-start(bf16[512,8,128]{0,2,1:T(8,128)(2,1)} %fusion.25) | copy-start | bytes 3145732
  276.8 129.2 %copy-start.10 = (bf16[1,128,5120]{2,1,0:T(8,128)(2,1)S(1)}, bf16[1,128,5120]{2,1,0:T(8,128)(2,1)}, u32[]{:S(2)}) copy-start(bf16[1,128,5120]{2,1,0:T(8,128)(2,1)} %param.18) | copy-start | bytes 3932164
  276.8 227.4 %all-gather.5.cloned.1.call-start = ((), (), s32[]{:S(2)}) async-start(), calls=%async_computation.11 | async-start | bytes 6553600 | tf_op jit(solution)/shard_map/all_gather | solution.py:188
  407.7 108.9 %copy-start.2 = (bf16[128,5120]{1,0:T(8,128)(2,1)}, bf16[128,5120]{1,0:T(8,128)(2,1)S(1)}, u32[]{:S(2)}) copy-start(bf16[128,5120]{1,0:T(8,128)(2,1)S(1)} %fusion.21) | copy-start | bytes 3932164
Sparse Core Ops, SparseCore 0:
  10.9 188.0 all-gather.2
  276.9 63.2 reduce-scatter.1
  443.3 60.8 all-gather.4
where the time goes:
time: 533 us; the launch traced here: 524 us
  waiting for transfers between devices  200 us (38%)
  matrix products  112 us (21%)
  local copies, waits for them, and re-layouts  85.2 us (16%)
  other arithmetic  41.9 us (8%)
  blocking collectives  35.4 us (7%)
  starting transfers between devices  32.9 us (6%)
  between operations  16.1 us (3%)
    all_to_all x1, waiting for transfers between devices, local(): lax.all_to_all(copies, 'dp', split_axis=0, concat_axis=0, tiled=True)  129 us
    all_gather x1, waiting for transfers between devices, local(): columns = lax.all_gather(columns, 'tensor', axis=0, tiled=True)  61 us
    unnamed x54, local copies, waits for them, and re-layouts  40.8 us
    all_to_all x1, blocking collectives, local(): lax.all_to_all(target.reshape(seq_local, clips, width), 'dp', split_axis=...  35.4 us
    dot_general x2, matrix products, attend_plain(): jnp.einsum('hqk,khd->qhd', rounded, value_rows, preferred_element_type=jn...  21 us
    another operation x2, other arithmetic  15.4 us
    sub x3, other arithmetic, softmax_rows(): exponent = jnp.exp(scores - row_peak)  15.2 us
    dot_general x1, matrix products, local(): jnp.einsum('csi,scd->cid', attended_all, columns, preferred_element_type=...  12.3 us
  transfers between devices with their start and end apart: 10, of which 4 were waited for; matrix products, arithmetic and copies ran while one was open for 41% of the time, Pallas kernels for 0%

commit v1 on v0

--- a/solution.py
+++ b/solution.py
@@ -8,6 +8,29 @@
 STEPS = 1000
 sigma_data = 0.5
 guidance = 5.0
+
+
+def split_up(value, dim, count):
+    shape = value.shape
+    blocks = value.reshape(*shape[:dim], count, shape[dim] // count, *shape[dim + 1 :])
+    return jnp.moveaxis(blocks, dim, 0)
+
+
+def joined_along(blocks, dim):
+    lengths = list(blocks.shape[1:])
+    lengths[dim] *= blocks.shape[0]
+    return jnp.moveaxis(blocks, 0, dim).reshape(lengths)
+
+
+def pairwise_exchange(x, axis, split_dim, concat_dim):
+    peers, here = (lax.axis_size(axis), lax.axis_index(axis))
+    tiles = split_up(x, split_dim, peers)
+    finished = [tiles[here]]
+    for turn in range(1, peers):
+        sent = tiles[here ^ turn]
+        finished.append(lax.ppermute(sent, axis, [(i, i ^ turn) for i in range(peers)]))
+    tiles = jnp.stack(finished)[here ^ jnp.arange(peers)]
+    return joined_along(tiles, concat_dim)
 
 
 def rope_angles(coords):
@@ -128,7 +151,7 @@
     )
     arrived = (
         lax.all_to_all(outgoing[0], "tensor", split_axis=1, concat_axis=0, tiled=True),
-        lax.all_to_all(outgoing[1], "tensor", split_axis=1, concat_axis=0, tiled=True),
+        pairwise_exchange(outgoing[1], "tensor", 1, 0),
         lax.all_to_all(outgoing[2], "tensor", split_axis=1, concat_axis=0, tiled=True),
         lax.all_to_all(outgoing[3], "tensor", split_axis=1, concat_axis=0, tiled=True),
         lax.all_to_all(outgoing[4], "tensor", split_axis=1, concat_axis=0, tiled=True),

time: 533 us -> 529 us (level)
  waiting for transfers between devices: 200 us -> 194 us
    sub x3, other arithmetic: 15.2 us -> 21.2 us  [softmax_rows(): exponent = jnp.exp(scores - row_peak)]
    all_to_all x1 -> x0, waiting for transfers between devices: 5.37 us -> none  [local(): lax.all_to_all(outgoing[1], 'tensor', split_axis=1, concat_axis=0, tiled=...]
    unnamed x54 -> x52, local copies, waits for them, and re-layouts: 40.8 us -> 39.1 us
    another operation x2 -> x3, other arithmetic: 15.4 us -> 14.4 us
  transfers between devices with their start and end apart: 10 -> 12, of which waited for: 4 -> 3; matrix products, arithmetic and copies ran while one was open for 41% -> 43% of each run, Pallas kernels for 0% -> 0%
where the time goes in v1:
time: 529 us; the launch traced here: 524 us
  waiting for transfers between devices  194 us (37%)
  matrix products  111 us (21%)
  local copies, waits for them, and re-layouts  87.4 us (17%)
  other arithmetic  46.7 us (9%)
  blocking collectives  35.4 us (7%)
  starting transfers between devices  33.1 us (6%)
  between operations  16.1 us (3%)
    all_to_all x1, waiting for transfers between devices, local(): lax.all_to_all(copies, 'dp', split_axis=0, concat_axis=0, tiled=True)  129 us
    all_gather x1, waiting for transfers between devices, local(): columns = lax.all_gather(columns, 'tensor', axis=0, tiled=True)  60.9 us
    unnamed x52, local copies, waits for them, and re-layouts  39.1 us
    all_to_all x1, blocking collectives, local(): lax.all_to_all(target.reshape(seq_local, clips, width), 'dp', split_axis=...  35.4 us
    dot_general x2, matrix products, attend_plain(): jnp.einsum('hqk,khd->qhd', rounded, value_rows, preferred_element_type=jn...  21.4 us
    sub x3, other arithmetic, softmax_rows(): exponent = jnp.exp(scores - row_peak)  21.2 us
    another operation x2, other arithmetic  13.2 us
    dot_general x1, matrix products, local(): jnp.einsum('csi,scd->cid', attended_all, columns, preferred_element_type=...  12.3 us
  transfers between devices with their start and end apart: 12, of which 3 were waited for; matrix products, arithmetic and copies ran while one was open for 43% of the time, Pallas kernels for 0%

profile of v1, /device:TPU:0, one launch (start us, length us, event | category | flops | bytes accessed | tf_op | source)
XLA Modules:
  0.0 524.2 jit_solution(2118055370871124230)
XLA Ops:
  7.2 3.6 pad_maximum_fusion
  19.8 6.3 %subtract_convert_fusion.5 = (bf16[128,32,64]{0,2,1:T(8,128)(2,1)}, bf16[128,32,64]{0,2,1:T(8,128)(2,1)}, bf16[128,32,64]{0,2,1:T(8,128)(2,1)S(1)}, bf16[128,32,...) fusion(f32[128,32,128]{0,2,1:T(8,128)} %bitcast.112, ...), kind=kLoop, calls=%fused_computation.78 | loop fusion | flops 8388608 | bytes 12648448 | tf_op jit(solution)/shard_map/convert.16
  35.0 4.6 all-to-all-start.2
  66.3 3.2 copy.194
  69.5 3.2 copy.195
  75.8 3.2 copy.197
  82.2 6.9 %subtract_convert_fusion = (bf16[512,8,64]{2,0,1:T(8,128)(2,1)S(1)}, bf16[512,8,64]{2,0,1:T(8,128)(2,1)S(1)}, bf16[512,8,64]{2,0,1:T(8,128)(2,1)S(1)}, bf16[512,...) fusion(f32[512,8,64]{2,0,1:T(8,128)} %copy.198, ...), kind=kLoop, calls=%fused_computation.42 | loop fusion | flops 8388608 | bytes 12845056 | tf_op jit(solution)/shard_map/convert.8
  90.3 4.6 fusion.30
  94.9 4.7 fusion.37
  99.6 4.9 all-to-all-start
  117.2 8.0 %fusion.98 = f32[8,512]{1,0:T(8,128)S(1)} fusion(f32[8,512,512]{1,2,0:T(8,128)} %fusion.30), kind=kOutput, calls=%fused_computation.134 | output fusion | flops 8389119 | bytes 8404992 | tf_op jit(solution)/shard_map/sub | solution.py:85
  125.2 4.3 all-to-all-start.3
  129.6 8.1 %fusion.99 = f32[8,512]{1,0:T(8,128)S(1)} fusion(f32[8,512,512]{1,2,0:T(8,128)} %fusion.37), kind=kOutput, calls=%fused_computation.135 | output fusion | flops 8389119 | bytes 8404992 | tf_op jit(solution)/shard_map/sub | solution.py:85
  137.6 3.9 all-to-all-done.3
  141.5 4.4 all-to-all-start.1
  146.0 10.6 %fusion.19 = f32[8,512,128]{1,2,0:T(8,128)} fusion(bf16[512,8,128]{0,2,1:T(8,128)(2,1)} %bitcast.134, f32[8,512]{1,0:T(8,128)S(1)} %fusion.98, f32[8,512,512]{1,2,0:T(8,128)} %fusion.30), kind=kOutput, calls=%fused_computation.31 | convolution fusion | flops 547361280 | bytes 11550720 | tf_op jit(solution)/shard_map/hqk,khd->qhd/dot_general | solution.py:94
  156.5 10.8 %fusion.25 = bf16[512,8,128]{0,2,1:T(8,128)(2,1)} fusion(f32[8,512,128]{1,2,0:T(8,128)} %fusion.19, f32[]{:T(128)} %bitcast.33, pred[]{:T(512)} %bitcast.34, bf16[512,8,128]{0,2,1:T(8,128)(2,1)S(1)} %bitcast.132, f32[8,512]{1,0:T(8,128)S(1)} %fusion.99, f32[8,512,512]{1,2,0:T(8,128)} %fusion.37), kind=kOutput, calls=%fused_computation.40 | convolution fusion | flops 551031296 | bytes 12599301 | tf_op jit(solution)/shard_map/hqk,khd->qhd/dot_general | solution.py:94
  179.9 4.5 all-to-all-start.4
  190.8 5.1 fusion.100
  196.7 10.9 %fusion.101 = (bf16[8,512,128]{1,2,0:T(8,128)(2,1)}, f32[8,512,128]{1,2,0:T(8,128)}) fusion(bf16[512,8,128]{0,2,1:T(8,128)(2,1)} %reshape.320, f32[8,512]{1,0:T(8,128)S(1)} %get-tuple-element.60, f32[8,512,512]{1,2,0:T(8,128)} %copy-done), kind=kOutput, calls=%fused_computation.137 | convolution fusion | flops 547885568 | bytes 12599296 | tf_op jit(solution)/shard_map/hqk,khd->qhd/dot_general | solution.py:105
  207.6 4.4 fusion.45
  212.1 5.1 broadcast_in_dim.28
  217.2 5.5 %all-to-all-start.5 = ((bf16[8,512,1024]{1,2,0:T(8,128)(2,1)}), bf16[8,512,1024]{1,2,0:T(8,128)(2,1)}, u32[]{:S(2)}, u32[]{:S(2)}) async-start(bf16[8,512,1024]{1,2,0:T(8,128)(2,1)} %broadcast_in_dim.28), calls=%async_computation.6 | async-start | bytes 16777216 | tf_op jit(solution)/shard_map/all_to_all | solution.py:199
  222.7 10.0 %multiply_reduce_fusion = (f32[8,512]{1,0:T(8,128)S(1)}, f32[8,512,512]{1,2,0:T(8,128)}) fusion(f32[8,512,512]{1,2,0:T(8,128)} %get-tuple-element.61, f32[8,512]{1,0:T(8,128)S(1)} %get-tuple-element.60, f32[8,512,512]{1,2,0:T(8,128)} %fusion.45, bf16[512,8,128]{2,1,0:T(8,128)(2,1)S(1)} %bitcast.133, bf16[512,8,128]{2,1,0:T(8,128)(2,1)S(1)} %bitcast.118), kind=kOutput, calls=%fused_computation.16 | convolution fusion | flops 547352576 | bytes 27295744 | tf_op jit(solution)/shard_map/qhd,khd->hqk/dot_general | solution.py:108
  235.2 10.2 %fusion.28 = f32[8,512,128]{1,2,0:T(8,128)} fusion(bf16[512,8,128]{0,2,1:T(8,128)(2,1)S(1)} %reshape.323, f32[8,512]{1,0:T(8,128)S(1)} %get-tuple-element.60, f32[8,512,512]{1,2,0:T(8,128)} %copy-done), kind=kOutput, calls=%fused_computation.52 | convolution fusion | flops 547361280 | bytes 11550720 | tf_op jit(solution)/shard_map/hqk,khd->qhd/dot_general | solution.py:114
  245.4 11.3 %subtract_convert_fusion.4 = bf16[8,512,128]{1,2,0:T(8,128)(2,1)S(1)} fusion(f32[8,512,128]{1,2,0:T(8,128)} %fusion.28, f32[8,512,128]{1,2,0:T(8,128)} %get-tuple-element.65, bf16[512,8,128]{0,2,1:T(8,128)(2,1)S(1)} %copy-done.13, f32[8,512,512]{1,2,0:T(8,128)} %get-tuple-element.63, f32[8,512]{1,0:T(8,128)S(1)} %get-tuple-element.62, f32[]{:T(128)S(6)} %mul.409, ...), kind=kOutput, calls=%fused_computation.49 | convolution fusion | flops 554177024 | bytes 23101448 | tf_op jit(solution)/shard_map/hqk,khd->qhd/dot_general | solution.py:112
  256.7 8.4 %fusion.3 = f32[512,5120]{1,0:T(8,128)S(1)} fusion(bf16[512,1024]{0,1:T(8,128)(2,1)S(1)} %bitcast.128, bf16[2,1024,5120]{2,1,0:T(8,128)(2,1)} %all-gather.3.cloned.1.call-done), kind=kOutput, calls=%fused_computation.7 | convolution fusion | flops 5368709120 | bytes 22020096 | tf_op jit(solution)/shard_map/dot_general | solution.py:193
  265.1 11.9 %add_convert_fusion = bf16[512,5120]{1,0:T(8,128)(2,1)} fusion(f32[512,5120]{1,0:T(8,128)S(1)} %fusion.3, bf16[512,1024]{0,1:T(8,128)(2,1)S(1)} %bitcast.136, bf16[2,1024,5120]{2,1,0:T(8,128)(2,1)} %all-gather.3.cloned.1.call-done), kind=kOutput, calls=%fused_computation.10 | convolution fusion | flops 5373952000 | bytes 27262976 | tf_op jit(solution)/shard_map/dot_general | solution.py:193
  277.4 129.2 %all-to-all-done.5 = bf16[8,512,1024]{1,2,0:T(8,128)(2,1)} async-done(((bf16[8,512,1024]{1,2,0:T(8,128)(2,1)}), bf16[8,512,1024]{1,2,0:T(8,128)(2,1)}, u32[]{:S(2)}, u32[]{:S(2)}) %all-to-all-start.5) | async-done | bytes 8388640 | tf_op jit(solution)/shard_map/all_to_all | solution.py:199
  408.5 35.4 %all_to_all.81 = bf16[128,8,640]{2,0,1:T(8,128)(2,1)} all-to-all(bf16[128,8,640]{2,0,1:T(8,128)(2,1)S(1)} %bitcast.116), channel_id=1, replica_groups=mesh['dp'=8,'tensor'=4] {'dp'}, dimensions={1} | all-to-all | bytes 2621440 | tf_op jit(solution)/shard_map/all_to_all | solution.py:208
  443.9 60.9 %all-gather.5.cloned.1.call-done = bf16[512,8,640]{2,0,1:T(8,128)(2,1)} async-done(((bf16[128,8,640]{2,0,1:T(8,128)(2,1)}), bf16[512,8,640]{2,0,1:T(8,128)(2,1)}) %all-gather.5.cloned.1.call-update) | async-done | bytes 5242896 | tf_op jit(solution)/shard_map/all_gather | solution.py:211
  504.8 12.3 %convert_reduce_fusion = f32[1024,640]{1,0:T(8,128)} fusion(bf16[8,512,1024]{1,2,0:T(8,128)(2,1)} %all-to-all-done.5, bf16[512,8,640]{2,0,1:T(8,128)(2,1)} %all-gather.5.cloned.1.call-done), kind=kOutput, calls=%fused_computation.4 | convolution fusion | flops 5389025280 | bytes 16252928 | tf_op jit(solution)/shard_map/csi,scd->cid/dot_general | solution.py:213
  (110 shorter events, 87.7 us)
Async XLA Ops:
  7.2 3.6 copy-start.9
  7.2 249.5 %all-gather.3.cloned.1.call-start = ((), (), s32[]{:S(2)}) async-start(), calls=%async_computation.8 | async-start | bytes 23592960 | tf_op jit(solution)/shard_map/all_gather | solution.py:192
  11.4 5.4 %copy-start.10 = (bf16[1,128,4096]{2,1,0:T(8,128)(2,1)S(1)}, bf16[1,128,4096]{2,1,0:T(8,128)(2,1)}, u32[]{:S(2)}) copy-start(bf16[1,128,4096]{2,1,0:T(8,128)(2,1)} %param.23) | copy-start | bytes 3145732
  11.4 7.0 %copy-start.16 = (s32[1,3,512]{2,0,1:T(1,128)S(1)}, s32[1,3,512]{2,0,1:T(1,128)}, u32[]{:S(2)}) copy-start(s32[1,3,512]{2,0,1:T(1,128)} %param.17) | copy-start | bytes 18436
  26.0 13.6 %copy-start.15 = (f32[512,64]{0,1:T(8,128)S(1)}, f32[512,64]{0,1:T(8,128)}, u32[]{:S(2)}) copy-start(f32[512,64]{0,1:T(8,128)} %get-tuple-element.55) | copy-start | bytes 393220
  27.7 139.6 %collective-permute-start = (bf16[128,1024]{1,0:T(8,128)(2,1)}, bf16[128,1024]{1,0:T(8,128)(2,1)}, u32[]{:S(2)}, u32[]{:S(2)}) collective-permute-start(bf16[128,1024]{1,0:T(8,128)(2,1)} %bitcast.10), channel_id=1, source_target_pairs={{0,1},{1,0},{2,3},{3,2},{4,5},{5,4},{6,7},{7,6},{8,9},{9,8},{10,11... | collective-permute-start | bytes 786440 | tf_op jit(solution)/shard_map/ppermute | solution.py:31
  31.6 135.8 %collective-permute-start.1 = (bf16[128,1024]{1,0:T(8,128)(2,1)}, bf16[128,1024]{1,0:T(8,128)(2,1)}, u32[]{:S(2)}, u32[]{:S(2)}) collective-permute-start(bf16[128,1024]{1,0:T(8,128)(2,1)} %bitcast.12), channel_id=1, source_target_pairs={{0,2},{1,3},{2,0},{3,1},{4,6},{5,7},{6,4},{7,5},{8,10},{9,11},{10,... | collective-permute-start | bytes 786440 | tf_op jit(solution)/shard_map/ppermute | solution.py:31
  34.0 133.4 %collective-permute-start.2 = (bf16[128,1024]{1,0:T(8,128)(2,1)}, bf16[128,1024]{1,0:T(8,128)(2,1)}, u32[]{:S(2)}, u32[]{:S(2)}) collective-permute-start(bf16[128,1024]{1,0:T(8,128)(2,1)} %bitcast.14), channel_id=1, source_target_pairs={{0,3},{1,2},{2,1},{3,0},{4,7},{5,6},{6,5},{7,4},{8,11},{9,10},{10,... | collective-permute-start | bytes 786440 | tf_op jit(solution)/shard_map/ppermute | solution.py:31
  35.0 64.5 %all-to-all-start.2 = ((bf16[128,4,1024]{0,2,1:T(8,128)(2,1)}), bf16[128,4,1024]{0,2,1:T(8,128)(2,1)}, u32[]{:S(2)}, u32[]{:S(2)}) async-start(bf16[128,4,1024]{0,2,1:T(8,128)(2,1)} %bitcast.21), calls=%async_computation.2 | async-start | bytes 2097152 | tf_op jit(solution)/shard_map/all_to_all | solution.py:156
  75.8 6.4 %copy-start.8 = (f32[512,64]{1,0:T(8,128)S(1)}, f32[512,64]{1,0:T(8,128)}, u32[]{:S(2)}) copy-start(f32[512,64]{1,0:T(8,128)} %copy.167) | copy-start | bytes 393220
  82.2 7.0 %copy-start.4 = (bf16[128,32,64]{0,2,1:T(8,128)(2,1)S(1)}, bf16[128,32,64]{0,2,1:T(8,128)(2,1)}, u32[]{:S(2)}) copy-start(bf16[128,32,64]{0,2,1:T(8,128)(2,1)} %get-tuple-element.52) | copy-start | bytes 1572868
  82.2 7.0 %copy-start.5 = (bf16[128,32,64]{0,2,1:T(8,128)(2,1)S(1)}, bf16[128,32,64]{0,2,1:T(8,128)(2,1)}, u32[]{:S(2)}) copy-start(bf16[128,32,64]{0,2,1:T(8,128)(2,1)} %get-tuple-element.53) | copy-start | bytes 1572868
  99.6 7.4 %copy-start.11 = (bf16[128,1,1024]{0,2,1:T(8,128)(2,1)S(1)}, bf16[128,1,1024]{0,2,1:T(8,128)(2,1)}, u32[]{:S(2)}) copy-start(bf16[128,1,1024]{0,2,1:T(8,128)(2,1)} %get-tuple-element.28) | copy-start | bytes 786436
  99.6 25.7 %all-to-all-start = ((bf16[128,4,1024]{0,2,1:T(8,128)(2,1)}), bf16[128,4,1024]{0,2,1:T(8,128)(2,1)S(1)}, u32[]{:S(2)}, u32[]{:S(2)}) async-start(bf16[128,4,1024]{0,2,1:T(8,128)(2,1)} %bitcast.5), calls=%async_computation | async-start | bytes 2097152 | tf_op jit(solution)/shard_map/all_to_all | solution.py:153
  125.2 12.4 %copy-start.2 = (bf16[128,4,1024]{0,2,1:T(8,128)(2,1)}, bf16[128,4,1024]{0,2,1:T(8,128)(2,1)S(1)}, u32[]{:S(2)}) copy-start(bf16[128,4,1024]{0,2,1:T(8,128)(2,1)S(1)} %all-to-all-done) | copy-start | bytes 3145732
  125.2 16.3 %all-to-all-start.3 = ((bf16[128,4,1024]{0,2,1:T(8,128)(2,1)}), bf16[128,4,1024]{0,2,1:T(8,128)(2,1)S(1)}, u32[]{:S(2)}, u32[]{:S(2)}) async-start(bf16[128,4,1024]{0,2,1:T(8,128)(2,1)} %bitcast.24), calls=%async_computation.3 | async-start | bytes 2097152 | tf_op jit(solution)/shard_map/all_to_all | solution.py:157
  141.5 15.0 %copy-start.3 = (bf16[128,4,1024]{0,2,1:T(8,128)(2,1)}, bf16[128,4,1024]{0,2,1:T(8,128)(2,1)S(1)}, u32[]{:S(2)}) copy-start(bf16[128,4,1024]{0,2,1:T(8,128)(2,1)S(1)} %all-to-all-done.3) | copy-start | bytes 3145732
  141.5 38.3 %all-to-all-start.1 = ((bf16[128,4,1024]{0,2,1:T(8,128)(2,1)}), bf16[128,4,1024]{0,2,1:T(8,128)(2,1)}, u32[]{:S(2)}, u32[]{:S(2)}) async-start(bf16[128,4,1024]{0,2,1:T(8,128)(2,1)} %bitcast.17), calls=%async_computation.1 | async-start | bytes 2097152 | tf_op jit(solution)/shard_map/all_to_all | solution.py:155
  156.5 10.8 %copy-start.14 = (bf16[128,1,1024]{2,0,1:T(8,128)(2,1)S(1)}, bf16[128,1,1024]{2,0,1:T(8,128)(2,1)}, u32[]{:S(2)}) copy-start(bf16[128,1,1024]{2,0,1:T(8,128)(2,1)} %copy.142) | copy-start | bytes 786436
  179.9 32.2 %all-to-all-start.4 = ((bf16[128,4,1024]{0,2,1:T(8,128)(2,1)}), bf16[128,4,1024]{0,2,1:T(8,128)(2,1)}, u32[]{:S(2)}, u32[]{:S(2)}) async-start(bf16[128,4,1024]{0,2,1:T(8,128)(2,1)} %bitcast.122), calls=%async_computation.4 | async-start | bytes 2097152 | tf_op jit(solution)/shard_map/all_to_all | solution.py:158
  190.8 5.9 %copy-start = (f32[8,512,512]{1,2,0:T(8,128)}, f32[8,512,512]{1,2,0:T(8,128)S(1)}, u32[]{:S(2)}) copy-start(f32[8,512,512]{1,2,0:T(8,128)S(1)} %fusion.48) | copy-start | bytes 25165828
  217.2 5.5 %copy-start.12 = (bf16[64,8,8,128]{3,2,1,0:T(8,128)(2,1)S(1)}, bf16[64,8,8,128]{3,2,1,0:T(8,128)(2,1)}, u32[]{:S(2)}) copy-start(bf16[64,8,8,128]{3,2,1,0:T(8,128)(2,1)} %copy.203) | copy-start | bytes 3145732
  217.2 189.5 %all-to-all-start.5 = ((bf16[8,512,1024]{1,2,0:T(8,128)(2,1)}), bf16[8,512,1024]{1,2,0:T(8,128)(2,1)}, u32[]{:S(2)}, u32[]{:S(2)}) async-start(bf16[8,512,1024]{1,2,0:T(8,128)(2,1)} %broadcast_in_dim.28), calls=%async_computation.6 | async-start | bytes 16777216 | tf_op jit(solution)/shard_map/all_to_all | solution.py:199
  222.7 184.0 %reduce-scatter.2.cloned.1.call-start = ((), (), s32[]{:S(2)}) async-start(), calls=%async_computation.9 | async-start | bytes 6553600 | tf_op jit(solution)/shard_map/reduce_scatter | solution.py:200
  235.2 10.2 %copy-start.13 = (bf16[512,8,128]{0,2,1:T(8,128)(2,1)S(1)}, bf16[512,8,128]{0,2,1:T(8,128)(2,1)}, u32[]{:S(2)}) copy-start(bf16[512,8,128]{0,2,1:T(8,128)(2,1)} %reshape.320) | copy-start | bytes 3145732
  245.4 11.3 %copy-start.6 = (bf16[512,8,128]{0,2,1:T(8,128)(2,1)S(1)}, bf16[512,8,128]{0,2,1:T(8,128)(2,1)}, u32[]{:S(2)}) copy-start(bf16[512,8,128]{0,2,1:T(8,128)(2,1)} %fusion.25) | copy-start | bytes 3145732
  277.1 129.6 %copy-start.7 = (bf16[1,128,5120]{2,1,0:T(8,128)(2,1)S(1)}, bf16[1,128,5120]{2,1,0:T(8,128)(2,1)}, u32[]{:S(2)}) copy-start(bf16[1,128,5120]{2,1,0:T(8,128)(2,1)} %param.18) | copy-start | bytes 3932164
  277.1 227.7 %all-gather.5.cloned.1.call-start = ((), (), s32[]{:S(2)}) async-start(), calls=%async_computation.10 | async-start | bytes 6553600 | tf_op jit(solution)/shard_map/all_gather | solution.py:211
  408.4 108.8 %copy-start.1 = (bf16[128,5120]{1,0:T(8,128)(2,1)}, bf16[128,5120]{1,0:T(8,128)(2,1)S(1)}, u32[]{:S(2)}) copy-start(bf16[128,5120]{1,0:T(8,128)(2,1)S(1)} %fusion.21) | copy-start | bytes 3932164
Sparse Core Ops, SparseCore 0:
  10.9 188.0 all-gather.2
  277.2 63.3 reduce-scatter.1
  444.0 60.7 all-gather.4
